TPU v7x, 512 devices: a whole 4x4x16 slice. The times are simulated.
512 devices in a mesh: bond: 32 (over z, core), row: 16 (over y, x).
Axes of the slice: x: 4, y: 4, z: 16, core: 2. Of those that a mesh axis runs over, the one named last changes fastest.
Arguments:
- left_core: float32 [32, 384, 2, 384], P('bond', 'row'), may hold values from -1 to 2
- right_core: float32 [32, 384, 2, 384], P('bond', 'row'), may hold values from -1 to 2
- gate_angles: float32 [32, 6], P('bond'), may hold values from -3.140625 to 3.140625
- sketch: float32 [768, 384], P('bond'), may hold values from -0.21875 to 0.21875
Outputs:
- next_pair: float32 [32, 768, 768], P('bond', 'row')
All inputs are finite; a program needn't handle non-finite values.
Results may differ from a plain program's by a relative error of at most 0.0003.
Values sent between devices are 32-bit elements; how exact they have to be, the bound alone decides.
No kernel may reach another device: no remote copies, remote signals or barrier semaphores. Data moves between devices by JAX's collectives and lax.ppermute only.
A program may use at most 64 MiB of HBM per device.

v0:
```python
import jax
import jax.numpy as jnp
import numpy as np
from jax import lax
from jax.sharding import PartitionSpec as P

ITERS = 2


HIGHEST = lax.Precision.HIGHEST
PLANES = ((0, 1), (2, 3), (0, 2), (1, 3), (0, 3), (1, 2))


def from_behind(value, axis, steps):
    count = lax.axis_size(axis)
    initial, last = (max(0, -steps), min(count, count - steps))
    return lax.ppermute(value, axis, [(source, source + steps) for source in range(initial, last)])


def rotation(first_axis, second_axis, cosine, sine_value):
    unit = np.eye(4, dtype=np.float32)
    diag_part = np.outer(unit[first_axis], unit[first_axis]) + np.outer(
        unit[second_axis], unit[second_axis]
    )
    skew_part = np.outer(unit[second_axis], unit[first_axis]) - np.outer(
        unit[first_axis], unit[second_axis]
    )
    rest_part = np.eye(4, dtype=np.float32) - diag_part
    return (
        jnp.asarray(rest_part)
        + cosine * jnp.asarray(diag_part)
        + sine_value * jnp.asarray(skew_part)
    )


def build_gate(angles):
    gate_matrix = jnp.eye(4, dtype=jnp.float32)
    for number, plane in enumerate(PLANES):
        rotated = rotation(plane[0], plane[1], jnp.cos(angles[number]), jnp.sin(angles[number]))
        gate_matrix = jnp.dot(
            rotated, gate_matrix, precision=HIGHEST, preferred_element_type=jnp.float32
        )
    return gate_matrix


def apply_gate(two_site, gate_matrix):
    width = two_site.shape[1] // 2
    blocks = two_site.reshape(two_site.shape[0] // 2, 2, 2, width)
    mixed_gate = jnp.einsum(
        "pqtu,atuc->apqc", gate_matrix.reshape(2, 2, 2, 2), blocks, precision=HIGHEST
    )
    return mixed_gate.reshape(two_site.shape)


def matmul(left_side, right_side):
    return jnp.dot(left_side, right_side, precision=HIGHEST, preferred_element_type=jnp.float32)


def inner_rows(left_side, right_side):
    return lax.dot_general(
        left_side,
        right_side,
        (((0,), (0,)), ((), ())),
        precision=HIGHEST,
        preferred_element_type=jnp.float32,
    )


def orthonormal(sketched):
    gram_matrix = lax.psum(inner_rows(sketched, sketched), "row")
    chol_factor = jnp.linalg.cholesky(gram_matrix)
    return lax.linalg.triangular_solve(
        chol_factor, sketched, left_side=False, lower=True, transpose_a=True
    )


def on_device(left_core, right_core, gate_angles, sketch):
    width = left_core.shape[3]
    local_sites = left_core.shape[1]
    local_rows = 2 * local_sites
    left_matrix = left_core.reshape(local_rows, width)
    shard_part = lax.all_gather(right_core, "row", axis=1, tiled=True)
    count = shard_part.shape[1]
    two_site = matmul(left_matrix, shard_part.reshape(count, 2 * width))
    two_site = apply_gate(two_site, build_gate(gate_angles[0]))
    shard_part = lax.all_gather(sketch, "bond", axis=0, tiled=True)
    sketched = matmul(two_site, shard_part)
    ortho_basis = orthonormal(sketched)
    for repeat in range(ITERS):
        projected = lax.psum(inner_rows(two_site, ortho_basis), "row")
        ortho_basis = orthonormal(matmul(two_site, projected))
    carried = lax.psum_scatter(
        inner_rows(ortho_basis, two_site), "row", scatter_dimension=0, tiled=True
    )
    incoming = from_behind(carried, "bond", 1)
    incoming_matrix = incoming.reshape(local_rows, width)
    stacked_final = ortho_basis.reshape(local_sites, 2, width)
    shard_part = lax.all_gather(stacked_final, "row", axis=0, tiled=True)
    count = shard_part.shape[0]
    next_block = matmul(incoming_matrix, shard_part.reshape(count, 2 * width))
    return next_block[None]


def solution(mesh):
    return jax.shard_map(
        on_device,
        mesh=mesh,
        in_specs=(
            P("bond", "row", None, None),
            P("bond", "row", None, None),
            P("bond", None),
            P("bond", None),
        ),
        out_specs=P("bond", "row", None),
        check_vma=False,
    )
```

profile of v0, /device:TPU:1, one launch (start us, length us, event | category | flops | bytes accessed | tf_op | source)
XLA Modules:
  0.0 1194.6 jit_solution(12344548351591145168)
XLA Ops:
  8.1 1.5 fusion.124
  18.0 0.8 fusion.85
  18.9 0.9 fusion.86
  19.7 0.9 fusion.87
  20.6 0.9 fusion.88
  21.4 0.9 fusion.89
  22.3 0.9 fusion.90
  23.2 48.9 %all-gather.4.cloned.1.call-done = f32[1,384,2,384]{3,2,0,1:T(2,128)} async-done(((f32[1,24,2,384]{3,2,0,1:T(2,128)}), f32[1,384,2,384]{3,2,0,1:T(2,128)}) %all-gather.4.cloned.1.call-update) | async-done | bytes 1179664 | tf_op jit(solution)/shard_map/all_gather | solution.py:82
  72.1 1.3 copy.48
  74.3 0.8 fusion.2
  75.9 70.6 %all-gather.6.cloned.1.call-done = f32[768,384]{1,0:T(8,128)} async-done(((f32[24,384]{1,0:T(8,128)}), f32[768,384]{1,0:T(8,128)}) %all-gather.6.cloned.1.call-update) | async-done | bytes 1179664 | tf_op jit(solution)/shard_map/all_gather | solution.py:86
  146.4 2.0 fusion.125
  148.4 1.5 fusion.126
  150.5 110.5 %all-reduce.8.cloned.1.call-done = f32[384,384]{0,1:T(8,128)} async-done(((f32[384,384]{0,1:T(8,128)}), f32[384,384]{0,1:T(8,128)}) %all-reduce.8.cloned.1.call-update) | async-done | bytes 589840 | tf_op jit(solution)/shard_map/psum | solution.py:70
  260.9 1.4 copy.33
  262.4 11.7 cholesky.273
  274.2 9.8 custom-call.23
  284.6 11.7 cholesky.292
  296.3 9.9 custom-call.24
  306.8 11.7 cholesky.311
  318.5 0.7 compare_reduce_fusion.6
  321.9 6.1 while.6
  322.6 1.3 bitcast_dynamic-update-slice_fusion.6
  324.6 1.3 bitcast_dynamic-update-slice_fusion.6
  326.6 1.3 bitcast_dynamic-update-slice_fusion.6
  328.0 29.5 %custom-call.25 = f32[3,128,128]{1,2,0:T(8,128)S(1)} custom-call(f32[3,128,128]{2,1,0:T(8,128)S(1)} %get-tuple-element.27), custom_call_target="InvertDiagBlocksLowerTriangular" | custom-call | tf_op jit(solution)/shard_map/triangular_solve/custom-call.2 | solution.py:72
  358.5 2.2 fusion.22
  360.8 118.0 %all-reduce.10.cloned.1.call-done = f32[768,384]{1,0:T(8,128)} async-done(((f32[768,384]{1,0:T(8,128)}), f32[768,384]{1,0:T(8,128)}) %all-reduce.10.cloned.1.call-update) | async-done | bytes 1179664 | tf_op jit(solution)/shard_map/psum | solution.py:90
  478.8 2.0 fusion.127
  480.8 1.5 fusion.128
  482.5 114.7 %all-reduce.12.cloned.1.call-done = f32[384,384]{0,1:T(8,128)} async-done(((f32[384,384]{0,1:T(8,128)}), f32[384,384]{0,1:T(8,128)}) %all-reduce.12.cloned.1.call-update) | async-done | bytes 589840 | tf_op jit(solution)/shard_map/psum | solution.py:70
  597.3 1.4 copy.35
  598.7 11.7 cholesky.326
  610.5 9.8 custom-call.26
  620.9 11.7 cholesky.345
  632.7 10.2 custom-call.27
  643.4 11.7 cholesky.364
  659.1 6.1 while.7
  659.8 1.3 bitcast_dynamic-update-slice_fusion.7
  661.8 1.3 bitcast_dynamic-update-slice_fusion.7
  663.8 1.3 bitcast_dynamic-update-slice_fusion.7
  665.2 29.5 %custom-call.28 = f32[3,128,128]{1,2,0:T(8,128)S(1)} custom-call(f32[3,128,128]{2,1,0:T(8,128)S(1)} %get-tuple-element.28), custom_call_target="InvertDiagBlocksLowerTriangular" | custom-call | tf_op jit(solution)/shard_map/triangular_solve/custom-call.2 | solution.py:72
  695.7 2.2 fusion.28
  698.0 118.0 %all-reduce.14.cloned.1.call-done = f32[768,384]{1,0:T(8,128)} async-done(((f32[768,384]{1,0:T(8,128)}), f32[768,384]{1,0:T(8,128)}) %all-reduce.14.cloned.1.call-update) | async-done | bytes 1179664 | tf_op jit(solution)/shard_map/psum | solution.py:90
  816.0 2.0 fusion.129
  818.0 1.5 fusion.130
  819.7 114.8 %all-reduce.16.cloned.1.call-done = f32[384,384]{0,1:T(8,128)} async-done(((f32[384,384]{0,1:T(8,128)}), f32[384,384]{0,1:T(8,128)}) %all-reduce.16.cloned.1.call-update) | async-done | bytes 589840 | tf_op jit(solution)/shard_map/psum | solution.py:70
  934.5 1.4 copy.37
  935.9 11.7 cholesky.379
  947.7 9.8 custom-call.29
  958.1 11.7 cholesky.398
  969.9 10.0 custom-call.30
  980.4 11.7 cholesky.417
  996.1 6.1 while.8
  996.8 1.3 bitcast_dynamic-update-slice_fusion.8
  998.8 1.3 bitcast_dynamic-update-slice_fusion.8
  1000.8 1.3 bitcast_dynamic-update-slice_fusion.8
  1002.2 29.5 %custom-call.31 = f32[3,128,128]{1,2,0:T(8,128)S(1)} custom-call(f32[3,128,128]{2,1,0:T(8,128)S(1)} %get-tuple-element.29), custom_call_target="InvertDiagBlocksLowerTriangular" | custom-call | tf_op jit(solution)/shard_map/triangular_solve/custom-call.2 | solution.py:72
  1032.7 2.1 fusion.120
  1035.7 88.7 %reduce-scatter.4.cloned.1.call-done = f32[24,768]{1,0:T(8,128)} async-done(((f32[384,768]{1,0:T(8,128)}), f32[24,768]{1,0:T(8,128)}) %reduce-scatter.4.cloned.1.call-update) | async-done | bytes 73744
  1124.4 5.4 collective-permute-start
  1129.8 55.2 %all-gather.8.cloned.1.call-done = f32[384,2,384]{2,1,0:T(2,128)} async-done(((f32[24,2,384]{2,1,0:T(2,128)}), f32[384,2,384]{2,1,0:T(2,128)}) %all-gather.8.cloned.1.call-update) | async-done | bytes 1179664 | tf_op jit(solution)/shard_map/all_gather | solution.py:98
  1185.0 1.3 copy.50
  1186.4 1.5 convolution_bitcast_fusion
  (115 shorter events, 22.7 us)
Async XLA Ops:
  6.5 65.6 %all-gather.4.cloned.1.call-start = ((), (), s32[]{:S(2)}) async-start(), calls=%async_computation.1 | async-start | bytes 1253376 | tf_op jit(solution)/shard_map/all_gather | solution.py:82
  7.3 139.2 %all-gather.6.cloned.1.call-start = ((), (), s32[]{:S(2)}) async-start(), calls=%async_computation.2 | async-start | bytes 1216512 | tf_op jit(solution)/shard_map/all_gather | solution.py:86
  8.0 252.9 %all-reduce.8.cloned.1.call-start = ((), (), s32[]{:S(2)}) async-start(), calls=%async_computation.3 | async-start | bytes 1179648 | tf_op jit(solution)/shard_map/psum | solution.py:70
  73.4 0.9 copy-start.3
  149.9 328.8 %all-reduce.10.cloned.1.call-start = ((), (), s32[]{:S(2)}) async-start(), calls=%async_computation.4 | async-start | bytes 2359296 | tf_op jit(solution)/shard_map/psum | solution.py:90
  260.9 1.4 copy-start
  360.7 236.5 %all-reduce.12.cloned.1.call-start = ((), (), s32[]{:S(2)}) async-start(), calls=%async_computation.5 | async-start | bytes 1179648 | tf_op jit(solution)/shard_map/psum | solution.py:70
  482.3 333.7 %all-reduce.14.cloned.1.call-start = ((), (), s32[]{:S(2)}) async-start(), calls=%async_computation.6 | async-start | bytes 2359296 | tf_op jit(solution)/shard_map/psum | solution.py:90
  597.3 1.4 copy-start.1
  697.9 236.5 %all-reduce.16.cloned.1.call-start = ((), (), s32[]{:S(2)}) async-start(), calls=%async_computation.7 | async-start | bytes 1179648 | tf_op jit(solution)/shard_map/psum | solution.py:70
  819.5 304.9 %reduce-scatter.4.cloned.1.call-start = ((), (), s32[]{:S(2)}) async-start(), calls=%async_computation.9 | async-start | bytes 1253376
  934.5 1.4 copy-start.2
  1034.9 150.1 %all-gather.8.cloned.1.call-start = ((), (), s32[]{:S(2)}) async-start(), calls=%async_computation.8 | async-start | bytes 1253376 | tf_op jit(solution)/shard_map/all_gather | solution.py:98
  1124.4 62.0 %collective-permute-start = (f32[24,768]{1,0:T(8,128)}, f32[24,768]{1,0:T(8,128)S(1)}, u32[]{:S(2)}, u32[]{:S(2)}) collective-permute-start(f32[24,768]{1,0:T(8,128)} %reduce-scatter.4.cloned.1.call-done), channel_id=1, source_target_pairs={{0,16},{16,32},{32,48},{48,64},{64,80},{80,96},{96,112},{112,128},... | collective-permute-start | bytes 221192 | tf_op jit(solution)/shard_map/ppermute | solution.py:17
Sparse Core Ops, SparseCore 0:
  10.3 61.7 all-gather.3
  74.2 72.1 all-gather.5
  150.1 110.8 all-reduce.7
  360.9 117.8 all-reduce.9
  482.4 114.8 all-reduce.11
  698.1 117.8 all-reduce.13
  819.6 114.8 all-reduce.15
  1035.0 89.2 reduce-scatter.3
  1127.4 57.5 all-gather.7
where the time goes:
time: 1200 us; the launch traced here: 1190 us
  waiting for transfers between devices  841 us (70%)
  other arithmetic  259 us (22%)
  matrix products  31.1 us (3%)
  local copies, waits for them, and re-layouts  28.3 us (2%)
  between operations  28.1 us (2%)
    psum x3, waiting for transfers between devices, orthonormal(): gram_matrix = lax.psum(inner_rows(sketched, sketched), 'row')  340 us
    psum x2, waiting for transfers between devices, on_device(): projected = lax.psum(inner_rows(two_site, ortho_basis), 'row')  236 us
    another operation x32, other arithmetic, orthonormal(): chol_factor = jnp.linalg.cholesky(gram_matrix)  171 us
    unnamed x10, waiting for transfers between devices  90.2 us
    another operation x8, other arithmetic, orthonormal(): lax.linalg.triangular_solve(chol_factor, sketched, left_side=False, lower...  88.6 us
    all_gather x1, waiting for transfers between devices, on_device(): shard_part = lax.all_gather(sketch, 'bond', axis=0, tiled=True)  70.6 us
    all_gather x1, waiting for transfers between devices, on_device(): shard_part = lax.all_gather(stacked_final, 'row', axis=0, tiled=True)  55.2 us
    all_gather x1, waiting for transfers between devices, on_device(): shard_part = lax.all_gather(right_core, 'row', axis=1, tiled=True)  48.9 us
  transfers between devices with their start and end apart: 10, of which 9 were waited for; matrix products, arithmetic and copies ran while one was open for 1% of the time, Pallas kernels for 0%

commit v1 on v0

--- a/solution.py
+++ b/solution.py
@@ -67,7 +67,7 @@
 
 
 def orthonormal(sketched):
-    gram_matrix = lax.psum(inner_rows(sketched, sketched), "row")
+    gram_matrix = inner_rows(sketched, sketched)
     chol_factor = jnp.linalg.cholesky(gram_matrix)
     return lax.linalg.triangular_solve(
         chol_factor, sketched, left_side=False, lower=True, transpose_a=True
@@ -78,26 +78,24 @@
     width = left_core.shape[3]
     local_sites = left_core.shape[1]
     local_rows = 2 * local_sites
-    left_matrix = left_core.reshape(local_rows, width)
-    shard_part = lax.all_gather(right_core, "row", axis=1, tiled=True)
-    count = shard_part.shape[1]
-    two_site = matmul(left_matrix, shard_part.reshape(count, 2 * width))
+    both = jnp.stack([left_core[0], right_core[0]], axis=1)
+    both = lax.all_gather(both, "row", axis=0, tiled=True)
+    sites = both.shape[0]
+    left_matrix = both[:, 0].reshape(2 * sites, width)
+    right_matrix = both[:, 1].reshape(sites, 2 * width)
+    two_site = matmul(left_matrix, right_matrix)
     two_site = apply_gate(two_site, build_gate(gate_angles[0]))
-    shard_part = lax.all_gather(sketch, "bond", axis=0, tiled=True)
-    sketched = matmul(two_site, shard_part)
-    ortho_basis = orthonormal(sketched)
+    full_sketch = lax.all_gather(sketch, "bond", axis=0, tiled=True)
+    ortho_basis = orthonormal(matmul(two_site, full_sketch))
     for repeat in range(ITERS):
-        projected = lax.psum(inner_rows(two_site, ortho_basis), "row")
+        projected = inner_rows(two_site, ortho_basis)
         ortho_basis = orthonormal(matmul(two_site, projected))
-    carried = lax.psum_scatter(
-        inner_rows(ortho_basis, two_site), "row", scatter_dimension=0, tiled=True
-    )
+    start = lax.axis_index("row") * local_sites
+    my_columns = lax.dynamic_slice_in_dim(ortho_basis, start, local_sites, axis=1)
+    carried = inner_rows(my_columns, two_site)
     incoming = from_behind(carried, "bond", 1)
     incoming_matrix = incoming.reshape(local_rows, width)
-    stacked_final = ortho_basis.reshape(local_sites, 2, width)
-    shard_part = lax.all_gather(stacked_final, "row", axis=0, tiled=True)
-    count = shard_part.shape[0]
-    next_block = matmul(incoming_matrix, shard_part.reshape(count, 2 * width))
+    next_block = matmul(incoming_matrix, ortho_basis.reshape(sites, 2 * width))
     return next_block[None]
 
 

time: 1200 us -> 630 us (0.53)
  waiting for transfers between devices: 841 us -> 109 us
  matrix products: 31.1 us -> 98.8 us
  other arithmetic: 259 us -> 320 us
  local copies, waits for them, and re-layouts: 28.3 us -> 59.9 us
    psum x5 -> x0, waiting for transfers between devices: 576 us -> none  [the longest x3 340 us: orthonormal(): gram_matrix = lax.psum(inner_rows(sketched, sketched), 'row')]
    unnamed x10 -> x2, waiting for transfers between devices: 90.2 us -> 0.71 us
    all_gather x3 -> x2, waiting for transfers between devices: 175 us -> 108 us  [the longest x1 56.2 us: on_device(): full_sketch = lax.all_gather(sketch, 'bond', axis=0, tiled=True)]
    another operation x32, other arithmetic: 171 us -> 215 us  [orthonormal(): chol_factor = jnp.linalg.cholesky(gram_matrix)]
    another operation x12, matrix products: 3.06 us -> 19.9 us  [orthonormal(): chol_factor = jnp.linalg.cholesky(gram_matrix)]
    another operation x15, matrix products: 2.98 us -> 19.2 us  [orthonormal(): lax.linalg.triangular_solve(chol_factor, sketched, left_side=False, lower...]
    another operation x31 -> x32, local copies, waits for them, and re-layouts: 18.2 us -> 34.2 us  [orthonormal(): lax.linalg.triangular_solve(chol_factor, sketched, left_side=False, lower...]
    dot_general x6, matrix products: 11 us -> 25.5 us  [inner_rows(): lax.dot_general(left_side, right_side, (((0,), (0,)), ((), ())), precisio...]
  transfers between devices with their start and end apart: 10 -> 3, of which waited for: 9 -> 3; matrix products, arithmetic and copies ran while one was open for 1% -> 4% of each run, Pallas kernels for 0% -> 0%
where the time goes in v1:
time: 630 us; the launch traced here: 619 us
  other arithmetic  320 us (51%)
  waiting for transfers between devices  109 us (17%)
  matrix products  98.8 us (16%)
  local copies, waits for them, and re-layouts  59.9 us (10%)
  between operations  28.1 us (4%)
    another operation x32, other arithmetic, orthonormal(): chol_factor = jnp.linalg.cholesky(gram_matrix)  215 us
    another operation x8, other arithmetic, orthonormal(): lax.linalg.triangular_solve(chol_factor, sketched, left_side=False, lower...  99.6 us
    all_gather x1, waiting for transfers between devices, on_device(): full_sketch = lax.all_gather(sketch, 'bond', axis=0, tiled=True)  56.2 us
    all_gather x1, waiting for transfers between devices, on_device(): both = lax.all_gather(both, 'row', axis=0, tiled=True)  51.3 us
    another operation x32, local copies, waits for them, and re-layouts, orthonormal(): lax.linalg.triangular_solve(chol_factor, sketched, left_side=False, lower...  34.2 us
    dot_general x6, matrix products, inner_rows(): lax.dot_general(left_side, right_side, (((0,), (0,)), ((), ())), precisio...  25.5 us
    another operation x12, matrix products, orthonormal(): chol_factor = jnp.linalg.cholesky(gram_matrix)  19.9 us
    another operation x15, matrix products, orthonormal(): lax.linalg.triangular_solve(chol_factor, sketched, left_side=False, lower...  19.2 us
  transfers between devices with their start and end apart: 3, of which 3 were waited for; matrix products, arithmetic and copies ran while one was open for 4% of the time, Pallas kernels for 0%

profile of v1, /device:TPU:1, one launch (start us, length us, event | category | flops | bytes accessed | tf_op | source)
XLA Modules:
  0.0 618.9 jit_solution(4283182410846225504)
XLA Ops:
  23.8 51.3 %all-gather.3.cloned.1.call-done = f32[384,2,2,384]{3,2,0,1:T(2,128)} async-done(((f32[24,2,2,384]{3,2,0,1:T(2,128)}), f32[384,2,2,384]{3,2,0,1:T(2,128)}) %all-gather.3.cloned.1.call-update) | async-done | bytes 2359312 | tf_op jit(solution)/shard_map/all_gather | solution.py:82
  75.1 2.4 slice_bitcast_fusion
  78.3 4.1 convolution_bitcast_fusion
  82.4 10.3 %fusion = f32[384,384,2,2,1]{1,3,4,2,0:T(2,128)S(1)} fusion(f32[384,2,2,384,1]{3,0,2,1,4:T(8,128)S(1)} %convolution_bitcast_fusion, f32[2,2,2,2]{3,2,1,0:T(2,128)S(1)} %reshape.66), kind=kOutput, calls=%fused_computation.6 | convolution fusion | flops 28311552 | bytes 4718656 | tf_op jit(solution)/shard_map/pqtu,atuc->apqc/dot_general | solution.py:49
  92.9 56.2 %all-gather.5.cloned.1.call-done = f32[768,384]{1,0:T(8,128)} async-done(((f32[24,384]{1,0:T(8,128)}), f32[768,384]{1,0:T(8,128)}) %all-gather.5.cloned.1.call-update) | async-done | bytes 1179664 | tf_op jit(solution)/shard_map/all_gather | solution.py:88
  149.2 5.1 fusion.123
  154.3 2.9 fusion.124
  157.1 2.1 copy.28
  162.0 13.2 %cholesky.273 = f32[128,128]{1,0:T(8,128)} custom-call(f32[128,128]{1,0:T(8,128)} %cholesky.428), custom_call_target="Cholesky" | custom-call | tf_op jit(solution)/shard_map/jit(cholesky)/cholesky | solution.py:71
  178.3 20.6 %custom-call.23 = f32[1,128,128]{1,2,0:T(8,128)} custom-call(f32[1,128,128]{2,1,0:T(8,128)} %get-tuple-element.82), custom_call_target="InvertDiagBlocksLowerTriangular" | custom-call | tf_op jit(solution)/shard_map/jit(cholesky)/cholesky | solution.py:71
  199.0 1.8 constant_dynamic-update-slice_fusion.5
  203.3 13.2 %cholesky.292 = f32[128,128]{1,0:T(8,128)} custom-call(f32[128,128]{1,0:T(8,128)} %cholesky.432), custom_call_target="Cholesky" | custom-call | tf_op jit(solution)/shard_map/jit(cholesky)/cholesky | solution.py:71
  217.9 11.3 %custom-call.24 = f32[1,128,128]{1,2,0:T(8,128)} custom-call(f32[1,128,128]{2,1,0:T(8,128)} %get-tuple-element.79), custom_call_target="InvertDiagBlocksLowerTriangular" | custom-call | tf_op jit(solution)/shard_map/jit(cholesky)/cholesky | solution.py:71
  229.2 1.7 convolution_dynamic-update-slice_fusion.2
  230.9 1.9 convolution_subtract_fusion.11
  232.8 13.2 %cholesky.311 = f32[128,128]{1,0:T(8,128)} custom-call(f32[128,128]{1,0:T(8,128)} %convolution_subtract_fusion.11), custom_call_target="Cholesky" | custom-call | tf_op jit(solution)/shard_map/jit(cholesky)/cholesky | solution.py:71
  250.7 1.9 select_select_fusion.2
  253.3 10.6 %while.6 = (s32[]{:T(128)}, f32[384,384]{1,0:T(8,128)}, s32[3,2]{0,1:T(2,128)S(1)}, f32[3,128,128]{2,1,0:T(8,128)}, s32[]{:T(128)}) while((s32[]{:T(128)}, f32[384,384]{1,0:T(8,128)}, s32[3,2]{0,1:T(2,128)S(1)}, f32[3,128,128]{2,1,0:T(8,128)}, s32[]{:T(128)}) %tuple.72), condition=%wide.while_cond, body=%wide.while_body.sunk | while | flops 2 | bytes 132205 | solution.py:72
  254.0 2.9 bitcast_dynamic-update-slice_fusion.6
  257.5 2.9 bitcast_dynamic-update-slice_fusion.6
  261.1 2.8 bitcast_dynamic-update-slice_fusion.6
  263.9 31.3 %custom-call.25 = f32[3,128,128]{1,2,0:T(8,128)} custom-call(f32[3,128,128]{2,1,0:T(8,128)} %get-tuple-element.27), custom_call_target="InvertDiagBlocksLowerTriangular" | custom-call | tf_op jit(solution)/shard_map/triangular_solve/custom-call.2 | solution.py:72
  298.8 2.3 convolution_subtract_fusion.5
  301.7 7.5 %fusion.2 = f32[768,384]{1,0:T(8,128)S(1)} fusion(f32[768,768]{1,0:T(8,128)S(1)} %bitcast.182, f32[768,128]{0,1:T(8,128)S(1)} %fusion.58, f32[768,128]{0,1:T(8,128)S(1)} %fusion.59, f32[768,128]{0,1:T(8,128)S(1)} %bitcast.189), kind=kOutput, calls=%fused_computation.16 | convolution fusion | flops 2718498816 | bytes 4718592 | tf_op jit(solution)/shard_map/dot_general | solution.py:60
  309.2 4.0 fusion.125
  313.2 2.9 fusion.126
  316.1 2.1 copy.29
  321.0 13.2 %cholesky.326 = f32[128,128]{1,0:T(8,128)} custom-call(f32[128,128]{1,0:T(8,128)} %cholesky.436), custom_call_target="Cholesky" | custom-call | tf_op jit(solution)/shard_map/jit(cholesky)/cholesky | solution.py:71
  335.6 1.7 cholesky.352
  337.3 11.3 %custom-call.26 = f32[1,128,128]{1,2,0:T(8,128)} custom-call(f32[1,128,128]{2,1,0:T(8,128)} %get-tuple-element.75), custom_call_target="InvertDiagBlocksLowerTriangular" | custom-call | tf_op jit(solution)/shard_map/jit(cholesky)/cholesky | solution.py:71
  348.6 1.8 constant_dynamic-update-slice_fusion.3
  352.9 13.4 %cholesky.345 = f32[128,128]{1,0:T(8,128)} custom-call(f32[128,128]{1,0:T(8,128)} %cholesky.440), custom_call_target="Cholesky" | custom-call | tf_op jit(solution)/shard_map/jit(cholesky)/cholesky | solution.py:71
  367.7 11.3 %custom-call.27 = f32[1,128,128]{1,2,0:T(8,128)} custom-call(f32[1,128,128]{2,1,0:T(8,128)} %get-tuple-element.72), custom_call_target="InvertDiagBlocksLowerTriangular" | custom-call | tf_op jit(solution)/shard_map/jit(cholesky)/cholesky | solution.py:71
  379.0 1.7 convolution_dynamic-update-slice_fusion.1
  380.7 1.9 convolution_subtract_fusion.10
  382.6 13.2 %cholesky.364 = f32[128,128]{1,0:T(8,128)} custom-call(f32[128,128]{1,0:T(8,128)} %convolution_subtract_fusion.10), custom_call_target="Cholesky" | custom-call | tf_op jit(solution)/shard_map/jit(cholesky)/cholesky | solution.py:71
  401.1 1.9 select_select_fusion.1
  403.8 10.6 %while.7 = (s32[]{:T(128)}, f32[384,384]{1,0:T(8,128)}, s32[3,2]{0,1:T(2,128)S(1)}, f32[3,128,128]{2,1,0:T(8,128)}, s32[]{:T(128)}) while((s32[]{:T(128)}, f32[384,384]{1,0:T(8,128)}, s32[3,2]{0,1:T(2,128)S(1)}, f32[3,128,128]{2,1,0:T(8,128)}, s32[]{:T(128)}) %tuple.85), condition=%wide.while_cond.clone, body=%wide.while_body.clone.sunk | while | flops 2 | bytes 132205 | solution.py:72
  404.4 2.9 bitcast_dynamic-update-slice_fusion.7
  408.0 2.9 bitcast_dynamic-update-slice_fusion.7
  411.5 2.8 bitcast_dynamic-update-slice_fusion.7
  414.3 31.3 %custom-call.28 = f32[3,128,128]{1,2,0:T(8,128)} custom-call(f32[3,128,128]{2,1,0:T(8,128)} %get-tuple-element.28), custom_call_target="InvertDiagBlocksLowerTriangular" | custom-call | tf_op jit(solution)/shard_map/triangular_solve/custom-call.2 | solution.py:72
  449.3 2.3 convolution_subtract_fusion.4
  452.1 7.5 %fusion.8 = f32[768,384]{1,0:T(8,128)S(1)} fusion(f32[768,768]{1,0:T(8,128)S(1)} %bitcast.184, f32[768,128]{0,1:T(8,128)S(1)} %fusion.53, f32[768,128]{0,1:T(8,128)S(1)} %fusion.54, f32[768,128]{0,1:T(8,128)S(1)} %bitcast.191), kind=kOutput, calls=%fused_computation.22 | convolution fusion | flops 2718498816 | bytes 4718592 | tf_op jit(solution)/shard_map/dot_general | solution.py:60
  459.6 4.0 fusion.127
  463.6 2.9 fusion.128
  466.5 2.1 copy.30
  471.4 13.2 %cholesky.379 = f32[128,128]{1,0:T(8,128)} custom-call(f32[128,128]{1,0:T(8,128)} %cholesky.444), custom_call_target="Cholesky" | custom-call | tf_op jit(solution)/shard_map/jit(cholesky)/cholesky | solution.py:71
  487.7 11.3 %custom-call.29 = f32[1,128,128]{1,2,0:T(8,128)} custom-call(f32[1,128,128]{2,1,0:T(8,128)} %get-tuple-element.68), custom_call_target="InvertDiagBlocksLowerTriangular" | custom-call | tf_op jit(solution)/shard_map/jit(cholesky)/cholesky | solution.py:71
  499.0 1.8 constant_dynamic-update-slice_fusion.1
  503.3 13.4 %cholesky.398 = f32[128,128]{1,0:T(8,128)} custom-call(f32[128,128]{1,0:T(8,128)} %cholesky.448), custom_call_target="Cholesky" | custom-call | tf_op jit(solution)/shard_map/jit(cholesky)/cholesky | solution.py:71
  518.1 11.3 %custom-call.30 = f32[1,128,128]{1,2,0:T(8,128)} custom-call(f32[1,128,128]{2,1,0:T(8,128)} %get-tuple-element.65), custom_call_target="InvertDiagBlocksLowerTriangular" | custom-call | tf_op jit(solution)/shard_map/jit(cholesky)/cholesky | solution.py:71
  529.4 1.7 convolution_dynamic-update-slice_fusion
  531.1 1.9 convolution_subtract_fusion.9
  533.0 13.2 %cholesky.417 = f32[128,128]{1,0:T(8,128)} custom-call(f32[128,128]{1,0:T(8,128)} %convolution_subtract_fusion.9), custom_call_target="Cholesky" | custom-call | tf_op jit(solution)/shard_map/jit(cholesky)/cholesky | solution.py:71
  551.5 1.9 select_select_fusion
  554.2 10.6 %while.8 = (s32[]{:T(128)}, f32[384,384]{1,0:T(8,128)}, s32[3,2]{0,1:T(2,128)S(1)}, f32[3,128,128]{2,1,0:T(8,128)}, s32[]{:T(128)}) while((s32[]{:T(128)}, f32[384,384]{1,0:T(8,128)}, s32[3,2]{0,1:T(2,128)S(1)}, f32[3,128,128]{2,1,0:T(8,128)}, s32[]{:T(128)}) %tuple.86), condition=%wide.while_cond.clone.1, body=%wide.while_body.clone.1.sunk | while | flops 2 | bytes 132205 | solution.py:72
  554.8 2.9 bitcast_dynamic-update-slice_fusion.8
  558.4 2.9 bitcast_dynamic-update-slice_fusion.8
  561.9 2.8 bitcast_dynamic-update-slice_fusion.8
  564.7 31.1 %custom-call.31 = f32[3,128,128]{1,2,0:T(8,128)} custom-call(f32[3,128,128]{2,1,0:T(8,128)} %get-tuple-element.29), custom_call_target="InvertDiagBlocksLowerTriangular" | custom-call | tf_op jit(solution)/shard_map/triangular_solve/custom-call.2 | solution.py:72
  599.5 2.3 convolution_subtract_fusion.3
  602.5 1.9 fusion.46
  604.3 3.2 collective-permute-start
  (106 shorter events, 71.9 us)
Async XLA Ops:
  6.5 68.6 %all-gather.3.cloned.1.call-start = ((), (), s32[]{:S(2)}) async-start(), calls=%async_computation | async-start | bytes 2506752 | tf_op jit(solution)/shard_map/all_gather | solution.py:82
  8.2 141.0 %all-gather.5.cloned.1.call-start = ((), (), s32[]{:S(2)}) async-start(), calls=%async_computation.1 | async-start | bytes 1216512 | tf_op jit(solution)/shard_map/all_gather | solution.py:88
  160.5 0.8 copy-start
  202.0 0.7 copy-start.3
  295.2 3.1 copy-start.6
  319.5 0.8 copy-start.1
  351.6 0.7 copy-start.4
  445.6 3.1 copy-start.7
  469.9 0.8 copy-start.2
  502.0 0.7 copy-start.5
  595.9 3.1 copy-start.8
  604.3 4.9 collective-permute-start
Sparse Core Ops, SparseCore 0:
  10.3 64.7 all-gather.2
  77.2 71.9 all-gather.4

commit v2 on v1

--- a/solution.py
+++ b/solution.py
@@ -2,6 +2,8 @@
 import jax.numpy as jnp
 import numpy as np
 from jax import lax
+from jax.experimental import pallas as pl
+from jax.experimental.pallas import tpu as pltpu
 from jax.sharding import PartitionSpec as P
 
 ITERS = 2
@@ -66,11 +68,68 @@
     )
 
 
+def pick_row(ref, base, offset, lanes):
+    tile = ref[pl.ds(base, 8), lanes]
+    sub = lax.broadcasted_iota(jnp.int32, tile.shape, 0)
+    return jnp.sum(jnp.where(sub == offset, tile, 0.0), axis=0, keepdims=True)
+
+
+def chol_inv_kernel(a_ref, w_ref, s_ref):
+    n = a_ref.shape[0]
+    s_ref[...] = a_ref[...]
+    rows = lax.broadcasted_iota(jnp.int32, (n, n), 0)
+    cols = lax.broadcasted_iota(jnp.int32, (n, n), 1)
+    w_ref[...] = jnp.where(rows == cols, 1.0, 0.0).astype(jnp.float32)
+    for q in range(n // 128):
+        r0 = q * 128
+        m = n - r0
+        wl = r0 + 128
+
+        def step(j, carry):
+            base = pl.multiple_of((j // 8) * 8, 8)
+            offset = j - base
+            srow = pick_row(s_ref, base, offset, slice(r0, n))
+            lane = lax.broadcasted_iota(jnp.int32, (1, m), 1) + r0
+            d = jnp.sum(jnp.where(lane == j, srow, 0.0), axis=1, keepdims=True)
+            r = lax.rsqrt(d)
+            v_s = jnp.where(lane > j, srow * r, 0.0)
+            v_w = pick_row(w_ref, base, offset, slice(0, wl)) * r
+            scol = s_ref[r0:n, r0:r0 + 128]
+            lane_c = lax.broadcasted_iota(jnp.int32, (m, 128), 1) + r0
+            col = jnp.sum(jnp.where(lane_c == j, scol, 0.0), axis=1, keepdims=True)
+            row_id = lax.broadcasted_iota(jnp.int32, (m, 1), 0) + r0
+            l_col = jnp.where(row_id > j, col * r, 0.0)
+            s_ref[r0:n, r0:n] = s_ref[r0:n, r0:n] - l_col * v_s
+            w_ref[r0:n, 0:wl] = w_ref[r0:n, 0:wl] - l_col * v_w
+            tile = w_ref[pl.ds(base, 8), 0:wl]
+            sub = lax.broadcasted_iota(jnp.int32, tile.shape, 0)
+            w_ref[pl.ds(base, 8), 0:wl] = jnp.where(sub == offset, v_w, tile)
+            return carry
+
+        lax.fori_loop(r0, r0 + 128, step, 0)
+
+
+def chol_inv(gram):
+    n = gram.shape[0]
+    return pl.pallas_call(
+        chol_inv_kernel,
+        out_shape=jax.ShapeDtypeStruct((n, n), jnp.float32),
+        in_specs=[pl.BlockSpec(memory_space=pltpu.VMEM)],
+        out_specs=pl.BlockSpec(memory_space=pltpu.VMEM),
+        scratch_shapes=[pltpu.VMEM((n, n), jnp.float32)],
+    )(gram)
+
+
 def orthonormal(sketched):
     gram_matrix = inner_rows(sketched, sketched)
-    chol_factor = jnp.linalg.cholesky(gram_matrix)
-    return lax.linalg.triangular_solve(
-        chol_factor, sketched, left_side=False, lower=True, transpose_a=True
+    gram_matrix = 0.5 * (gram_matrix + gram_matrix.T)
+    inverse_factor = chol_inv(gram_matrix)
+    return lax.dot_general(
+        sketched,
+        inverse_factor,
+        (((1,), (1,)), ((), ())),
+        precision=HIGHEST,
+        preferred_element_type=jnp.float32,
     )
 
 

time: 630 us -> 416 us (0.66)
  other arithmetic: 320 us -> 8.03 us
  Pallas kernels: 0 us -> 193 us
  local copies, waits for them, and re-layouts: 59.9 us -> 13.3 us
  matrix products: 98.8 us -> 61.7 us
    another operation x40 -> x0, other arithmetic: 314 us -> none  [the longest x32 215 us: orthonormal(): chol_factor = jnp.linalg.cholesky(gram_matrix)]
    pallas_call x0 -> x3, Pallas kernels: none -> 193 us  [chol_inv(): pl.pallas_call(chol_inv_kernel, out_shape=jax.ShapeDtypeStruct((n, n), jn...]
    another operation x41 -> x0, local copies, waits for them, and re-layouts: 43 us -> none  [the longest x32 34.2 us: orthonormal(): lax.linalg.triangular_solve(chol_factor, sketched, left_side=False, lower...]
    another operation x27 -> x0, matrix products: 39.1 us -> none  [the longest x12 19.9 us: orthonormal(): chol_factor = jnp.linalg.cholesky(gram_matrix)]
    dot_general x0 -> x3, matrix products: none -> 10 us  [orthonormal(): lax.dot_general(sketched, inverse_factor, (((1,), (1,)), ((), ())), preci...]
    dot_general x6, matrix products: 25.5 us -> 18 us  [inner_rows(): lax.dot_general(left_side, right_side, (((0,), (0,)), ((), ())), precisio...]
    mul x0 -> x3, other arithmetic: none -> 6.39 us  [orthonormal(): gram_matrix = 0.5 * (gram_matrix + gram_matrix.T)]
  transfers between devices with their start and end apart: 3 -> 3, of which waited for: 3 -> 2; matrix products, arithmetic and copies ran while one was open for 4% -> 6% of each run, Pallas kernels for 0% -> 0%
where the time goes in v2:
time: 416 us; the launch traced here: 410 us
  Pallas kernels  193 us (46%)
  waiting for transfers between devices  108 us (26%)
  matrix products  61.7 us (15%)
  between operations  22.3 us (5%)
  local copies, waits for them, and re-layouts  13.3 us (3%)
  other arithmetic  8.03 us (2%)
    pallas_call x3, Pallas kernels, chol_inv(): pl.pallas_call(chol_inv_kernel, out_shape=jax.ShapeDtypeStruct((n, n), jn...  193 us
    all_gather x1, waiting for transfers between devices, on_device(): full_sketch = lax.all_gather(sketch, 'bond', axis=0, tiled=True)  56.3 us
    all_gather x1, waiting for transfers between devices, on_device(): both = lax.all_gather(both, 'row', axis=0, tiled=True)  50.9 us
    dot_general x5, matrix products, matmul(): jnp.dot(left_side, right_side, precision=HIGHEST, preferred_element_type=...  18.4 us
    dot_general x6, matrix products, inner_rows(): lax.dot_general(left_side, right_side, (((0,), (0,)), ((), ())), precisio...  18 us
    dot_general x1, matrix products, apply_gate(): jnp.einsum('pqtu,atuc->apqc', gate_matrix.reshape(2, 2, 2, 2), blocks, pr...  10.3 us
    dot_general x3, matrix products, orthonormal(): lax.dot_general(sketched, inverse_factor, (((1,), (1,)), ((), ())), preci...  10 us
  transfers between devices with their start and end apart: 3, of which 2 were waited for; matrix products, arithmetic and copies ran while one was open for 6% of the time, Pallas kernels for 0%

profile of v2, /device:TPU:1, one launch (start us, length us, event | category | flops | bytes accessed | tf_op | source)
XLA Modules:
  0.0 409.6 jit_solution(4392900782470844237)
XLA Ops:
  6.5 0.0 all-gather.3.cloned.1.call-start
  6.5 1.6 pad_maximum_fusion
  8.2 0.0 all-gather.3.cloned.1.call-update
  8.2 0.0 all-gather.5.cloned.1.call-start
  8.3 0.7 all-gather.5.cloned.1.call-update
  9.0 1.6 fusion.42
  19.0 0.8 fusion.11
  19.8 0.9 fusion.12
  20.7 0.9 fusion.13
  21.5 0.9 fusion.14
  22.4 0.9 fusion.15
  23.2 0.9 fusion.16
  24.1 0.1 reshape.40
  24.2 50.9 %all-gather.3.cloned.1.call-done = f32[384,2,2,384]{3,2,0,1:T(2,128)} async-done(((f32[24,2,2,384]{3,2,0,1:T(2,128)}), f32[384,2,2,384]{3,2,0,1:T(2,128)}) %all-gather.3.cloned.1.call-update) | async-done | bytes 2359312 | tf_op jit(solution)/shard_map/all_gather | solution.py:141
  75.1 2.4 slice_bitcast_fusion
  77.5 0.1 copy.39
  77.6 0.6 reshape.45
  78.3 4.1 %convolution_bitcast_fusion = f32[384,2,2,384,1]{3,0,2,1,4:T(8,128)S(1)} fusion(f32[2,384,384,1]{1,0,2,3:T(2,128)S(1)} %reshape.45, f32[384,2,384,1]{2,1,0,3:T(2,128)S(1)} %get-tuple-element.5), kind=kOutput, calls=%fused_computation.2 | convolution fusion | flops 2717908992 | bytes 4718592 | tf_op jit(solution)/shard_map/dot_general | solution.py:58
  82.4 10.3 %fusion = f32[384,384,2,2,1]{1,3,4,2,0:T(2,128)S(1)} fusion(f32[384,2,2,384,1]{3,0,2,1,4:T(8,128)S(1)} %convolution_bitcast_fusion, f32[2,2,2,2]{3,2,1,0:T(2,128)S(1)} %reshape.40), kind=kOutput, calls=%fused_computation | convolution fusion | flops 28311552 | bytes 4718656 | tf_op jit(solution)/shard_map/pqtu,atuc->apqc/dot_general | solution.py:51
  92.7 0.2 copy.40
  92.8 56.3 %all-gather.5.cloned.1.call-done = f32[768,384]{1,0:T(8,128)} async-done(((f32[24,384]{1,0:T(8,128)}), f32[768,384]{1,0:T(8,128)}) %all-gather.5.cloned.1.call-update) | async-done | bytes 1179664 | tf_op jit(solution)/shard_map/all_gather | solution.py:147
  149.1 5.1 %fusion.43 = f32[768,384]{1,0:T(8,128)S(1)} fusion(f32[768,768]{1,0:T(8,128)S(1)} %bitcast.81, f32[768,384]{1,0:T(8,128)} %all-gather.5.cloned.1.call-done), kind=kOutput, calls=%fused_computation.57 | convolution fusion | flops 2717908992 | bytes 4718592 | tf_op jit(solution)/shard_map/dot_general | solution.py:58
  154.2 2.9 fusion.44
  157.1 2.1 copy.28
  159.2 2.1 fusion.6.a_ref
  161.4 64.6 %shard_map.208 = f32[384,384]{1,0:T(8,128)} custom-call(f32[384,384]{1,0:T(8,128)} %fusion.6.a_ref), custom_call_target="tpu_custom_call" | custom-call | tf_op jit(solution)/shard_map/pallas_call | solution.py:114
  226.0 3.5 fusion.45
  229.5 3.9 fusion.46
  233.3 3.8 fusion.47
  237.2 3.1 fusion.48
  240.2 2.1 copy.29
  242.3 2.1 fusion.5.a_ref
  244.5 64.2 %shard_map.209 = f32[384,384]{1,0:T(8,128)} custom-call(f32[384,384]{1,0:T(8,128)} %fusion.5.a_ref), custom_call_target="tpu_custom_call" | custom-call | tf_op jit(solution)/shard_map/pallas_call | solution.py:114
  308.7 3.5 fusion.49
  312.2 3.9 fusion.50
  316.0 3.8 fusion.51
  319.9 3.1 fusion.52
  323.0 2.1 copy.30
  325.1 2.1 fusion.4.a_ref
  327.2 64.2 %shard_map.210 = f32[384,384]{1,0:T(8,128)} custom-call(f32[384,384]{1,0:T(8,128)} %fusion.4.a_ref), custom_call_target="tpu_custom_call" | custom-call | tf_op jit(solution)/shard_map/pallas_call | solution.py:114
  391.4 3.1 fusion.53
  394.6 0.0 copy-start
  394.6 1.2 fusion.7
  395.8 0.0 copy-done
  395.8 3.2 collective-permute-start
  399.1 1.6 copy.31
  400.7 0.3 reshape.43
  401.0 0.0 collective-permute-done
  401.1 1.5 convolution_bitcast_fusion.1
  (1 shorter events, 0.0 us)
Async XLA Ops:
  6.5 68.6 %all-gather.3.cloned.1.call-start = ((), (), s32[]{:S(2)}) async-start(), calls=%async_computation | async-start | bytes 2506752 | tf_op jit(solution)/shard_map/all_gather | solution.py:141
  8.2 140.9 %all-gather.5.cloned.1.call-start = ((), (), s32[]{:S(2)}) async-start(), calls=%async_computation.1 | async-start | bytes 1216512 | tf_op jit(solution)/shard_map/all_gather | solution.py:147
  394.6 1.2 copy-start
  395.8 5.2 %collective-permute-start = (f32[24,768]{1,0:T(8,128)S(1)}, f32[24,768]{1,0:T(8,128)S(1)}, u32[]{:S(2)}, u32[]{:S(2)}) collective-permute-start(f32[24,768]{1,0:T(8,128)S(1)} %fusion.7), channel_id=1, source_target_pairs={{0,16},{16,32},{32,48},{48,64},{64,80},{80,96},{96,112},{112,128},... | collective-permute-start | bytes 221192 | tf_op jit(solution)/shard_map/ppermute | solution.py:19
Sparse Core Ops, SparseCore 0:
  10.3 64.7 all-gather.2
  77.2 71.8 all-gather.4

commit v3 on v2

--- a/solution.py
+++ b/solution.py
@@ -133,6 +133,25 @@
     )
 
 
+def doubling_gather(block, axis):
+    count = lax.axis_size(axis)
+    index = lax.axis_index(axis)
+    bits = count.bit_length() - 1
+    gathered = block[None]
+    for bit in reversed(range(bits)):
+        mask = 1 << bit
+        received = lax.ppermute(gathered, axis, [(source, source ^ mask) for source in range(count)])
+        upper = (index & mask) != 0
+        gathered = jnp.where(
+            upper,
+            jnp.stack([received, gathered]),
+            jnp.stack([gathered, received]),
+        )
+    order = tuple(range(bits - 1, -1, -1)) + tuple(range(bits, gathered.ndim))
+    gathered = jnp.transpose(gathered, order)
+    return gathered.reshape((count * block.shape[0],) + block.shape[1:])
+
+
 def on_device(left_core, right_core, gate_angles, sketch):
     width = left_core.shape[3]
     local_sites = left_core.shape[1]
@@ -144,7 +163,7 @@
     right_matrix = both[:, 1].reshape(sites, 2 * width)
     two_site = matmul(left_matrix, right_matrix)
     two_site = apply_gate(two_site, build_gate(gate_angles[0]))
-    full_sketch = lax.all_gather(sketch, "bond", axis=0, tiled=True)
+    full_sketch = doubling_gather(sketch, "bond")
     ortho_basis = orthonormal(matmul(two_site, full_sketch))
     for repeat in range(ITERS):
         projected = inner_rows(two_site, ortho_basis)

time: 416 us -> 362 us (0.87)
  waiting for transfers between devices: 108 us -> 26 us
  starting transfers between devices: 3.29 us -> 29.6 us
    all_gather x1 -> x0, waiting for transfers between devices: 56.3 us -> none  [on_device(): full_sketch = lax.all_gather(sketch, 'bond', axis=0, tiled=True)]
    all_gather x1, waiting for transfers between devices: 50.9 us -> 0.01 us  [on_device(): both = lax.all_gather(both, 'row', axis=0, tiled=True)]
    ppermute x0 -> x5, starting transfers between devices: none -> 27.2 us  [doubling_gather(): lax.ppermute(gathered, axis, [(source, source ^ mask) for source in range...]
    ppermute x0 -> x5, waiting for transfers between devices: none -> 26 us  [doubling_gather(): lax.ppermute(gathered, axis, [(source, source ^ mask) for source in range...]
  transfers between devices with their start and end apart: 3 -> 7, of which waited for: 2 -> 3; matrix products, arithmetic and copies ran while one was open for 6% -> 3% of each run, Pallas kernels for 0% -> 0%
where the time goes in v3:
time: 362 us; the launch traced here: 355 us
  Pallas kernels  193 us (53%)
  matrix products  58.3 us (16%)
  starting transfers between devices  29.6 us (8%)
  waiting for transfers between devices  26 us (7%)
  between operations  22.5 us (6%)
  local copies, waits for them, and re-layouts  14.5 us (4%)
  other arithmetic  11.2 us (3%)
    pallas_call x3, Pallas kernels, chol_inv(): pl.pallas_call(chol_inv_kernel, out_shape=jax.ShapeDtypeStruct((n, n), jn...  193 us
    ppermute x5, starting transfers between devices, doubling_gather(): lax.ppermute(gathered, axis, [(source, source ^ mask) for source in range...  27.2 us
    ppermute x5, waiting for transfers between devices, doubling_gather(): lax.ppermute(gathered, axis, [(source, source ^ mask) for source in range...  26 us
    dot_general x6, matrix products, inner_rows(): lax.dot_general(left_side, right_side, (((0,), (0,)), ((), ())), precisio...  18 us
    dot_general x5, matrix products, matmul(): jnp.dot(left_side, right_side, precision=HIGHEST, preferred_element_type=...  17.1 us
    dot_general x1, matrix products, apply_gate(): jnp.einsum('pqtu,atuc->apqc', gate_matrix.reshape(2, 2, 2, 2), blocks, pr...  10.3 us
    dot_general x3, matrix products, orthonormal(): lax.dot_general(sketched, inverse_factor, (((1,), (1,)), ((), ())), preci...  10 us
  transfers between devices with their start and end apart: 7, of which 3 were waited for; matrix products, arithmetic and copies ran while one was open for 3% of the time, Pallas kernels for 0%

profile of v3, /device:TPU:1, one launch (start us, length us, event | category | flops | bytes accessed | tf_op | source)
XLA Modules:
  0.0 355.2 jit_solution(15146317079681530252)
XLA Ops:
  6.5 1.6 pad_maximum_fusion.2
  8.2 0.0 all-gather.2.cloned.1.call-update
  8.2 16.3 %collective-permute-start = (f32[1,24,384]{2,1,0:T(8,128)}, f32[1,24,384]{2,1,0:T(8,128)S(1)}, u32[]{:S(2)}, u32[]{:S(2)}) collective-permute-start(f32[1,24,384]{2,1,0:T(8,128)} %bitcast.143), channel_id=1, source_target_pairs={{0,256},{16,272},{32,288},{48,304},{64,320},{80,336},{96,352},{112... | collective-permute-start | bytes 110600 | tf_op jit(solution)/shard_map/ppermute | solution.py:143
  24.5 1.6 fusion.50
  30.3 0.8 fusion.19
  31.2 0.9 fusion.20
  32.0 0.9 fusion.21
  34.2 0.9 maximum_select_fusion.5
  35.1 4.0 %collective-permute-start.1 = (f32[2,1,24,384]{3,2,0,1:T(8,128)S(1)}, f32[2,1,24,384]{3,2,0,1:T(8,128)S(1)}, u32[]{:S(2)}, u32[]{:S(2)}) collective-permute-start(f32[2,1,24,384]{3,2,0,1:T(8,128)S(1)} %maximum_select_fusion.5), channel_id=1, source_target_pairs={{0,128},{16,144},{32,160},{48,176},{64,192},{80,208},{96,224},{112... | collective-permute-start | bytes 221192 | tf_op jit(solution)/shard_map/ppermute | solution.py:143
  39.1 0.9 fusion.15
  39.9 9.4 %collective-permute-done.1 = f32[2,1,24,384]{3,2,0,1:T(8,128)S(1)} collective-permute-done((f32[2,1,24,384]{3,2,0,1:T(8,128)S(1)}, f32[2,1,24,384]{3,2,0,1:T(8,128)S(1)}, u32[]{:S(2)}, u32[]{:S(2)}) %collective-permute-start.1) | collective-permute-done | bytes 73760 | tf_op jit(solution)/shard_map/ppermute | solution.py:143
  49.3 1.9 collective-permute-start.2
  51.3 8.7 %collective-permute-done.2 = f32[2,2,1,24,384]{4,3,0,1,2:T(8,128)S(1)} collective-permute-done((f32[2,2,1,24,384]{4,3,0,1,2:T(8,128)S(1)}, f32[2,2,1,24,384]{4,3,0,1,2:T(8,128)S(1)}, u32[]{:S(2)}, u32[]{:S(2)}) %collective-permute-start.2) | collective-permute-done | bytes 147488 | tf_op jit(solution)/shard_map/ppermute | solution.py:143
  60.0 1.9 collective-permute-start.3
  62.0 0.0 copy-start.4
  62.0 0.0 copy-start.5
  62.0 0.0 copy-start.8
  62.0 0.0 copy-start.2
  62.0 0.0 copy-start.3
  62.0 0.0 copy-start.7
  62.1 0.0 copy-start.6
  62.1 8.0 %collective-permute-done.3 = f32[2,2,2,1,24,384]{5,4,0,1,2,3:T(8,128)S(1)} collective-permute-done((f32[2,2,2,1,24,384]{5,4,0,1,2,3:T(8,128)S(1)}, f32[2,2,2,1,24,384]{5,4,0,1,2,3:T(8,128)S(1)}, u32[]{:S(2)}, u32[]{:S(2)}) %collective-permute-start.3) | collective-permute-done | bytes 294944 | tf_op jit(solution)/shard_map/ppermute | solution.py:143
  70.1 3.2 collective-permute-start.4
  73.3 0.1 fusion.22
  76.3 0.1 fusion.23
  76.4 0.1 fusion.24
  76.6 0.1 reshape.1087
  76.7 0.1 fusion.4
  76.7 0.0 collective-permute-done.4
  76.8 1.1 maximum_select_fusion
  77.9 2.4 slice_bitcast_fusion
  80.4 0.1 copy.51
  80.4 0.6 reshape.1093
  81.1 4.1 %convolution_bitcast_fusion = f32[384,2,2,384,1]{3,0,2,1,4:T(8,128)S(1)} fusion(f32[2,384,384,1]{1,0,2,3:T(2,128)S(1)} %reshape.1093, f32[384,2,384,1]{2,1,0,3:T(2,128)S(1)} %get-tuple-element.5), kind=kOutput, calls=%fused_computation.2 | convolution fusion | flops 2717908992 | bytes 4718592 | tf_op jit(solution)/shard_map/dot_general | solution.py:58
  85.2 10.3 %fusion = f32[384,384,2,2,1]{1,3,4,2,0:T(2,128)S(1)} fusion(f32[384,2,2,384,1]{3,0,2,1,4:T(8,128)S(1)} %convolution_bitcast_fusion, f32[2,2,2,2]{3,2,1,0:T(2,128)S(1)} %reshape.1087), kind=kOutput, calls=%fused_computation | convolution fusion | flops 28311552 | bytes 4718656 | tf_op jit(solution)/shard_map/pqtu,atuc->apqc/dot_general | solution.py:51
  95.5 0.2 copy.52
  95.7 1.1 copy-done.1
  96.8 3.8 %fusion.51 = f32[768,384]{1,0:T(8,128)S(1)} fusion(f32[768,768]{1,0:T(8,128)S(1)} %bitcast.126, f32[768,384]{1,0:T(8,128)S(1)} %bitcast.134), kind=kOutput, calls=%fused_computation.80 | convolution fusion | flops 2717908992 | bytes 4718592 | tf_op jit(solution)/shard_map/dot_general | solution.py:58
  100.6 2.9 fusion.52
  103.5 2.1 copy.40
  105.6 2.1 fusion.7.a_ref
  107.8 64.6 %shard_map.208 = f32[384,384]{1,0:T(8,128)} custom-call(f32[384,384]{1,0:T(8,128)} %fusion.7.a_ref), custom_call_target="tpu_custom_call" | custom-call | tf_op jit(solution)/shard_map/pallas_call | solution.py:114
  172.4 3.5 fusion.53
  175.9 3.9 %fusion.54 = f32[768,384]{1,0:T(8,128)S(1)} fusion(f32[768,768]{1,0:T(8,128)S(1)} %bitcast.127, f32[768,384]{1,0:T(8,128)S(1)} %fusion.53), kind=kOutput, calls=%fused_computation.83 | convolution fusion | flops 2717908992 | bytes 4718592 | tf_op jit(solution)/shard_map/dot_general | solution.py:62
  179.7 3.8 %fusion.55 = f32[768,384]{1,0:T(8,128)S(1)} fusion(f32[768,768]{1,0:T(8,128)S(1)} %bitcast.128, f32[768,384]{1,0:T(8,128)S(1)} %fusion.54), kind=kOutput, calls=%fused_computation.84 | convolution fusion | flops 2717908992 | bytes 4718592 | tf_op jit(solution)/shard_map/dot_general | solution.py:58
  183.6 3.1 fusion.56
  186.6 2.1 copy.41
  188.8 2.1 fusion.6.a_ref
  190.9 64.2 %shard_map.209 = f32[384,384]{1,0:T(8,128)} custom-call(f32[384,384]{1,0:T(8,128)} %fusion.6.a_ref), custom_call_target="tpu_custom_call" | custom-call | tf_op jit(solution)/shard_map/pallas_call | solution.py:114
  255.1 3.5 fusion.57
  258.6 3.9 %fusion.58 = f32[768,384]{1,0:T(8,128)S(1)} fusion(f32[768,768]{1,0:T(8,128)S(1)} %bitcast.129, f32[768,384]{1,0:T(8,128)S(1)} %fusion.57), kind=kOutput, calls=%fused_computation.87 | convolution fusion | flops 2717908992 | bytes 4718592 | tf_op jit(solution)/shard_map/dot_general | solution.py:62
  262.5 3.8 %fusion.59 = f32[768,384]{1,0:T(8,128)S(1)} fusion(f32[768,768]{1,0:T(8,128)S(1)} %bitcast.130, f32[768,384]{1,0:T(8,128)S(1)} %fusion.58), kind=kOutput, calls=%fused_computation.88 | convolution fusion | flops 2717908992 | bytes 4718592 | tf_op jit(solution)/shard_map/dot_general | solution.py:58
  266.3 3.1 fusion.60
  269.4 2.1 copy.42
  271.5 2.1 fusion.5.a_ref
  273.7 64.2 %shard_map.210 = f32[384,384]{1,0:T(8,128)} custom-call(f32[384,384]{1,0:T(8,128)} %fusion.5.a_ref), custom_call_target="tpu_custom_call" | custom-call | tf_op jit(solution)/shard_map/pallas_call | solution.py:114
  337.9 3.1 fusion.61
  341.0 1.2 fusion.11
  342.3 0.0 copy-done
  342.3 2.4 collective-permute-start.5
  344.7 1.6 copy.43
  346.3 0.3 reshape.1091
  346.7 0.0 collective-permute-done.5
  346.7 1.5 convolution_bitcast_fusion.1
  (21 shorter events, 0.3 us)
Async XLA Ops:
  6.5 71.4 %all-gather.2.cloned.1.call-start = ((), (), s32[]{:S(2)}) async-start(), calls=%async_computation | async-start | bytes 2506752 | tf_op jit(solution)/shard_map/all_gather | solution.py:160
  8.2 26.0 %collective-permute-start = (f32[1,24,384]{2,1,0:T(8,128)}, f32[1,24,384]{2,1,0:T(8,128)S(1)}, u32[]{:S(2)}, u32[]{:S(2)}) collective-permute-start(f32[1,24,384]{2,1,0:T(8,128)} %bitcast.143), channel_id=1, source_target_pairs={{0,256},{16,272},{32,288},{48,304},{64,320},{80,336},{96,352},{112... | collective-permute-start | bytes 110600 | tf_op jit(solution)/shard_map/ppermute | solution.py:143
  35.1 14.3 %collective-permute-start.1 = (f32[2,1,24,384]{3,2,0,1:T(8,128)S(1)}, f32[2,1,24,384]{3,2,0,1:T(8,128)S(1)}, u32[]{:S(2)}, u32[]{:S(2)}) collective-permute-start(f32[2,1,24,384]{3,2,0,1:T(8,128)S(1)} %maximum_select_fusion.5), channel_id=1, source_target_pairs={{0,128},{16,144},{32,160},{48,176},{64,192},{80,208},{96,224},{112... | collective-permute-start | bytes 221192 | tf_op jit(solution)/shard_map/ppermute | solution.py:143
  49.3 10.6 %collective-permute-start.2 = (f32[2,2,1,24,384]{4,3,0,1,2:T(8,128)S(1)}, f32[2,2,1,24,384]{4,3,0,1,2:T(8,128)S(1)}, u32[]{:S(2)}, u32[]{:S(2)}) collective-permute-start(f32[2,2,1,24,384]{4,3,0,1,2:T(8,128)S(1)} %maximum_select_fusion.4), channel_id=1, source_target_pairs={{0,64},{16,80},{32,96},{48,112},{64,0},{80,16},{96,32},{112,48},{1... | collective-permute-start | bytes 442376 | tf_op jit(solution)/shard_map/ppermute | solution.py:143
  60.0 10.1 %collective-permute-start.3 = (f32[2,2,2,1,24,384]{5,4,0,1,2,3:T(8,128)S(1)}, f32[2,2,2,1,24,384]{5,4,0,1,2,3:T(8,128)S(1)}, u32[]{:S(2)}, u32[]{:S(2)}) collective-permute-start(f32[2,2,2,1,24,384]{5,4,0,1,2,3:T(8,128)S(1)} %maximum_select_fusion.3), channel_id=1, source_target_pairs={{0,32},{16,48},{32,0},{48,16},{64,96},{80,112},{96,64},{112,80},{1... | collective-permute-start | bytes 884744 | tf_op jit(solution)/shard_map/ppermute | solution.py:143
  62.0 11.3 %copy-start.4 = (f32[4,4]{1,0:T(4,128)S(1)}, f32[4,4]{1,0:T(4,128)}, u32[]{:S(2)}) copy-start(f32[4,4]{1,0:T(4,128)} %constant.56.clone) | copy-start | bytes 196
  62.0 11.3 %copy-start.5 = (f32[4,4]{1,0:T(4,128)S(1)}, f32[4,4]{1,0:T(4,128)}, u32[]{:S(2)}) copy-start(f32[4,4]{1,0:T(4,128)} %constant.55.clone) | copy-start | bytes 196
  62.0 11.3 %copy-start.8 = (f32[4,4]{1,0:T(4,128)S(1)}, f32[4,4]{1,0:T(4,128)}, u32[]{:S(2)}) copy-start(f32[4,4]{1,0:T(4,128)} %constant.58.clone) | copy-start | bytes 196
  62.0 14.3 %copy-start.2 = (f32[4,4]{1,0:T(4,128)S(1)}, f32[4,4]{1,0:T(4,128)}, u32[]{:S(2)}) copy-start(f32[4,4]{1,0:T(4,128)} %constant.60.clone) | copy-start | bytes 196
  62.0 14.3 %copy-start.3 = (f32[4,4]{1,0:T(4,128)S(1)}, f32[4,4]{1,0:T(4,128)}, u32[]{:S(2)}) copy-start(f32[4,4]{1,0:T(4,128)} %constant.59.clone) | copy-start | bytes 196
  62.0 14.3 %copy-start.7 = (f32[4,4]{1,0:T(4,128)S(1)}, f32[4,4]{1,0:T(4,128)}, u32[]{:S(2)}) copy-start(f32[4,4]{1,0:T(4,128)} %constant.61.clone) | copy-start | bytes 196
  62.1 14.4 %copy-start.6 = (f32[4,4]{1,0:T(4,128)S(1)}, f32[4,4]{1,0:T(4,128)}, u32[]{:S(2)}) copy-start(f32[4,4]{1,0:T(4,128)} %constant.62.clone) | copy-start | bytes 196
  70.1 6.6 %collective-permute-start.4 = (f32[2,2,2,2,1,24,384]{6,5,1,2,3,4,0:T(8,128)S(1)}, f32[2,2,2,2,1,24,384]{6,5,1,2,3,4,0:T(8,128)S(1)}, u32[]{:S(2)}, u32[]{:S(2)}) collective-permute-start(f32[2,2,2,2,1,24,384]{6,5,1,2,3,4,0:T(8,128)S(1)} %maximum_select_fusion.1), channel_id=1, source_target_pairs={{0,16},{16,0},{32,48},{48,32},{64,80},{80,64},{96,112},{112,96},{1... | collective-permute-start | bytes 1769480 | tf_op jit(solution)/shard_map/ppermute | solution.py:143
  95.5 1.3 copy-start.1
  341.0 1.2 copy-start
  342.3 4.4 %collective-permute-start.5 = (f32[24,768]{1,0:T(8,128)S(1)}, f32[24,768]{1,0:T(8,128)S(1)}, u32[]{:S(2)}, u32[]{:S(2)}) collective-permute-start(f32[24,768]{1,0:T(8,128)S(1)} %fusion.11), channel_id=1, source_target_pairs={{0,16},{16,32},{32,48},{48,64},{64,80},{80,96},{96,112},{112,128},... | collective-permute-start | bytes 221192 | tf_op jit(solution)/shard_map/ppermute | solution.py:19
Sparse Core Ops, SparseCore 0:
  10.3 64.6 all-gather.1

commit v4 on v3

--- a/solution.py
+++ b/solution.py
@@ -68,45 +68,74 @@
     )
 
 
+BLOCK = 128
+
+
 def pick_row(ref, base, offset, lanes):
     tile = ref[pl.ds(base, 8), lanes]
     sub = lax.broadcasted_iota(jnp.int32, tile.shape, 0)
     return jnp.sum(jnp.where(sub == offset, tile, 0.0), axis=0, keepdims=True)
 
 
+def block_dot(left_side, right_side):
+    return jnp.dot(left_side, right_side, precision=HIGHEST, preferred_element_type=jnp.float32)
+
+
 def chol_inv_kernel(a_ref, w_ref, s_ref):
     n = a_ref.shape[0]
+    nb = BLOCK
+    blocks = n // nb
     s_ref[...] = a_ref[...]
-    rows = lax.broadcasted_iota(jnp.int32, (n, n), 0)
-    cols = lax.broadcasted_iota(jnp.int32, (n, n), 1)
-    w_ref[...] = jnp.where(rows == cols, 1.0, 0.0).astype(jnp.float32)
-    for q in range(n // 128):
-        r0 = q * 128
+    w_ref[...] = jnp.zeros((n, n), jnp.float32)
+    eye_rows = lax.broadcasted_iota(jnp.int32, (nb, nb), 0)
+    eye_cols = lax.broadcasted_iota(jnp.int32, (nb, nb), 1)
+    eye = jnp.where(eye_rows == eye_cols, 1.0, 0.0).astype(jnp.float32)
+    for p in range(blocks):
+        r0 = p * nb
         m = n - r0
-        wl = r0 + 128
+        w_ref[r0:r0 + nb, r0:r0 + nb] = eye
 
         def step(j, carry):
             base = pl.multiple_of((j // 8) * 8, 8)
             offset = j - base
-            srow = pick_row(s_ref, base, offset, slice(r0, n))
-            lane = lax.broadcasted_iota(jnp.int32, (1, m), 1) + r0
+            srow = pick_row(s_ref, base, offset, slice(r0, r0 + nb))
+            lane = lax.broadcasted_iota(jnp.int32, (1, nb), 1) + r0
             d = jnp.sum(jnp.where(lane == j, srow, 0.0), axis=1, keepdims=True)
             r = lax.rsqrt(d)
-            v_s = jnp.where(lane > j, srow * r, 0.0)
-            v_w = pick_row(w_ref, base, offset, slice(0, wl)) * r
-            scol = s_ref[r0:n, r0:r0 + 128]
-            lane_c = lax.broadcasted_iota(jnp.int32, (m, 128), 1) + r0
-            col = jnp.sum(jnp.where(lane_c == j, scol, 0.0), axis=1, keepdims=True)
+            l_row = jnp.where(lane > j, srow * r, 0.0)
+            panel = s_ref[r0:n, r0:r0 + nb]
+            lane_p = lax.broadcasted_iota(jnp.int32, (m, nb), 1) + r0
+            col = jnp.sum(jnp.where(lane_p == j, panel, 0.0), axis=1, keepdims=True)
             row_id = lax.broadcasted_iota(jnp.int32, (m, 1), 0) + r0
-            l_col = jnp.where(row_id > j, col * r, 0.0)
-            s_ref[r0:n, r0:n] = s_ref[r0:n, r0:n] - l_col * v_s
-            w_ref[r0:n, 0:wl] = w_ref[r0:n, 0:wl] - l_col * v_w
-            tile = w_ref[pl.ds(base, 8), 0:wl]
-            sub = lax.broadcasted_iota(jnp.int32, tile.shape, 0)
-            w_ref[pl.ds(base, 8), 0:wl] = jnp.where(sub == offset, v_w, tile)
+            scaled = col * r
+            l_col = jnp.where(row_id > j, scaled, 0.0)
+            l_keep = jnp.where(row_id >= j, scaled, 0.0)
+            s_ref[r0:n, r0:r0 + nb] = jnp.where(lane_p == j, l_keep, panel - l_col * l_row)
+            w_row = pick_row(w_ref, base, offset, slice(r0, r0 + nb)) * r
+            w_block = w_ref[r0:r0 + nb, r0:r0 + nb]
+            sub = lax.broadcasted_iota(jnp.int32, (nb, nb), 0) + r0
+            w_block = jnp.where(sub == j, w_row, w_block - l_col[:nb] * w_row)
+            w_ref[r0:r0 + nb, r0:r0 + nb] = w_block
             return carry
 
-        lax.fori_loop(r0, r0 + 128, step, 0)
+        lax.fori_loop(r0, r0 + nb, step, 0)
+        if p + 1 < blocks:
+            below = s_ref[r0 + nb:n, r0:r0 + nb]
+            s_ref[r0 + nb:n, r0 + nb:n] = s_ref[r0 + nb:n, r0 + nb:n] - lax.dot_general(
+                below, below, (((1,), (1,)), ((), ())),
+                precision=HIGHEST, preferred_element_type=jnp.float32,
+            )
+    for a in range(1, blocks):
+        for b in range(a - 1, -1, -1):
+            acc = jnp.zeros((nb, nb), jnp.float32)
+            for k in range(b, a):
+                acc = acc + block_dot(
+                    s_ref[a * nb:(a + 1) * nb, k * nb:(k + 1) * nb],
+                    w_ref[k * nb:(k + 1) * nb, b * nb:(b + 1) * nb],
+                )
+            w_ref[a * nb:(a + 1) * nb, b * nb:(b + 1) * nb] = -block_dot(
+                w_ref[a * nb:(a + 1) * nb, a * nb:(a + 1) * nb], acc
+            )
 
 
 def chol_inv(gram):
@@ -118,7 +147,6 @@
         out_specs=pl.BlockSpec(memory_space=pltpu.VMEM),
         scratch_shapes=[pltpu.VMEM((n, n), jnp.float32)],
     )(gram)
-
 
 def orthonormal(sketched):
     gram_matrix = inner_rows(sketched, sketched)

time: 362 us -> 354 us (0.978)
  Pallas kernels: 193 us -> 185 us
    pallas_call x3, Pallas kernels: 193 us -> 185 us  [chol_inv(): pl.pallas_call(chol_inv_kernel, out_shape=jax.ShapeDtypeStruct((n, n), jn...]
where the time goes in v4:
time: 354 us; the launch traced here: 348 us
  Pallas kernels  185 us (52%)
  matrix products  58.4 us (16%)
  starting transfers between devices  29.6 us (8%)
  waiting for transfers between devices  26 us (7%)
  between operations  22.5 us (6%)
  local copies, waits for them, and re-layouts  14.5 us (4%)
  other arithmetic  11.2 us (3%)
    pallas_call x3, Pallas kernels, chol_inv(): pl.pallas_call(chol_inv_kernel, out_shape=jax.ShapeDtypeStruct((n, n), jn...  185 us
    ppermute x5, starting transfers between devices, doubling_gather(): lax.ppermute(gathered, axis, [(source, source ^ mask) for source in range...  27.2 us
    ppermute x5, waiting for transfers between devices, doubling_gather(): lax.ppermute(gathered, axis, [(source, source ^ mask) for source in range...  26 us
    dot_general x6, matrix products, inner_rows(): lax.dot_general(left_side, right_side, (((0,), (0,)), ((), ())), precisio...  18.1 us
    dot_general x5, matrix products, matmul(): jnp.dot(left_side, right_side, precision=HIGHEST, preferred_element_type=...  17.1 us
    dot_general x1, matrix products, apply_gate(): jnp.einsum('pqtu,atuc->apqc', gate_matrix.reshape(2, 2, 2, 2), blocks, pr...  10.3 us
    dot_general x3, matrix products, orthonormal(): lax.dot_general(sketched, inverse_factor, (((1,), (1,)), ((), ())), preci...  10 us
  transfers between devices with their start and end apart: 7, of which 3 were waited for; matrix products, arithmetic and copies ran while one was open for 3% of the time, Pallas kernels for 0%

profile of v4, /device:TPU:1, one launch (start us, length us, event | category | flops | bytes accessed | tf_op | source)
XLA Modules:
  0.0 347.5 jit_solution(4228836923830824531)
XLA Ops:
  6.5 1.6 pad_maximum_fusion.2
  8.2 0.0 all-gather.2.cloned.1.call-update
  8.2 16.3 %collective-permute-start = (f32[1,24,384]{2,1,0:T(8,128)}, f32[1,24,384]{2,1,0:T(8,128)S(1)}, u32[]{:S(2)}, u32[]{:S(2)}) collective-permute-start(f32[1,24,384]{2,1,0:T(8,128)} %bitcast.143), channel_id=1, source_target_pairs={{0,256},{16,272},{32,288},{48,304},{64,320},{80,336},{96,352},{112... | collective-permute-start | bytes 110600 | tf_op jit(solution)/shard_map/ppermute | solution.py:171
  24.5 1.6 fusion.50
  30.3 0.8 fusion.19
  31.2 0.9 fusion.20
  32.0 0.9 fusion.21
  34.2 0.9 maximum_select_fusion.5
  35.1 4.0 %collective-permute-start.1 = (f32[2,1,24,384]{3,2,0,1:T(8,128)S(1)}, f32[2,1,24,384]{3,2,0,1:T(8,128)S(1)}, u32[]{:S(2)}, u32[]{:S(2)}) collective-permute-start(f32[2,1,24,384]{3,2,0,1:T(8,128)S(1)} %maximum_select_fusion.5), channel_id=1, source_target_pairs={{0,128},{16,144},{32,160},{48,176},{64,192},{80,208},{96,224},{112... | collective-permute-start | bytes 221192 | tf_op jit(solution)/shard_map/ppermute | solution.py:171
  39.1 0.9 fusion.15
  39.9 9.4 %collective-permute-done.1 = f32[2,1,24,384]{3,2,0,1:T(8,128)S(1)} collective-permute-done((f32[2,1,24,384]{3,2,0,1:T(8,128)S(1)}, f32[2,1,24,384]{3,2,0,1:T(8,128)S(1)}, u32[]{:S(2)}, u32[]{:S(2)}) %collective-permute-start.1) | collective-permute-done | bytes 73760 | tf_op jit(solution)/shard_map/ppermute | solution.py:171
  49.3 1.9 collective-permute-start.2
  51.3 8.7 %collective-permute-done.2 = f32[2,2,1,24,384]{4,3,0,1,2:T(8,128)S(1)} collective-permute-done((f32[2,2,1,24,384]{4,3,0,1,2:T(8,128)S(1)}, f32[2,2,1,24,384]{4,3,0,1,2:T(8,128)S(1)}, u32[]{:S(2)}, u32[]{:S(2)}) %collective-permute-start.2) | collective-permute-done | bytes 147488 | tf_op jit(solution)/shard_map/ppermute | solution.py:171
  60.0 1.9 collective-permute-start.3
  62.0 0.0 copy-start.4
  62.0 0.0 copy-start.5
  62.0 0.0 copy-start.8
  62.0 0.0 copy-start.2
  62.0 0.0 copy-start.3
  62.0 0.0 copy-start.7
  62.1 0.0 copy-start.6
  62.1 8.0 %collective-permute-done.3 = f32[2,2,2,1,24,384]{5,4,0,1,2,3:T(8,128)S(1)} collective-permute-done((f32[2,2,2,1,24,384]{5,4,0,1,2,3:T(8,128)S(1)}, f32[2,2,2,1,24,384]{5,4,0,1,2,3:T(8,128)S(1)}, u32[]{:S(2)}, u32[]{:S(2)}) %collective-permute-start.3) | collective-permute-done | bytes 294944 | tf_op jit(solution)/shard_map/ppermute | solution.py:171
  70.1 3.2 collective-permute-start.4
  73.3 0.1 fusion.22
  76.3 0.1 fusion.23
  76.4 0.1 fusion.24
  76.6 0.1 reshape.1087
  76.7 0.1 fusion.4
  76.7 0.0 collective-permute-done.4
  76.8 1.1 maximum_select_fusion
  77.9 2.4 slice_bitcast_fusion
  80.4 0.1 copy.51
  80.4 0.6 reshape.1093
  81.1 4.1 %convolution_bitcast_fusion = f32[384,2,2,384,1]{3,0,2,1,4:T(8,128)S(1)} fusion(f32[2,384,384,1]{1,0,2,3:T(2,128)S(1)} %reshape.1093, f32[384,2,384,1]{2,1,0,3:T(2,128)S(1)} %get-tuple-element.5), kind=kOutput, calls=%fused_computation.2 | convolution fusion | flops 2717908992 | bytes 4718592 | tf_op jit(solution)/shard_map/dot_general | solution.py:58
  85.2 10.3 %fusion = f32[384,384,2,2,1]{1,3,4,2,0:T(2,128)S(1)} fusion(f32[384,2,2,384,1]{3,0,2,1,4:T(8,128)S(1)} %convolution_bitcast_fusion, f32[2,2,2,2]{3,2,1,0:T(2,128)S(1)} %reshape.1087), kind=kOutput, calls=%fused_computation | convolution fusion | flops 28311552 | bytes 4718656 | tf_op jit(solution)/shard_map/pqtu,atuc->apqc/dot_general | solution.py:51
  95.5 0.2 copy.52
  95.7 1.1 copy-done.1
  96.8 3.8 %fusion.51 = f32[768,384]{1,0:T(8,128)S(1)} fusion(f32[768,768]{1,0:T(8,128)S(1)} %bitcast.126, f32[768,384]{1,0:T(8,128)S(1)} %bitcast.134), kind=kOutput, calls=%fused_computation.80 | convolution fusion | flops 2717908992 | bytes 4718592 | tf_op jit(solution)/shard_map/dot_general | solution.py:58
  100.6 2.9 fusion.52
  103.5 2.1 copy.40
  105.6 2.1 fusion.7.a_ref
  107.8 62.0 %shard_map.208 = f32[384,384]{1,0:T(8,128)} custom-call(f32[384,384]{1,0:T(8,128)} %fusion.7.a_ref), custom_call_target="tpu_custom_call" | custom-call | tf_op jit(solution)/shard_map/pallas_call | solution.py:143
  169.8 3.5 fusion.53
  173.3 3.9 %fusion.54 = f32[768,384]{1,0:T(8,128)S(1)} fusion(f32[768,768]{1,0:T(8,128)S(1)} %bitcast.127, f32[768,384]{1,0:T(8,128)S(1)} %fusion.53), kind=kOutput, calls=%fused_computation.83 | convolution fusion | flops 2717908992 | bytes 4718592 | tf_op jit(solution)/shard_map/dot_general | solution.py:62
  177.1 3.8 %fusion.55 = f32[768,384]{1,0:T(8,128)S(1)} fusion(f32[768,768]{1,0:T(8,128)S(1)} %bitcast.128, f32[768,384]{1,0:T(8,128)S(1)} %fusion.54), kind=kOutput, calls=%fused_computation.84 | convolution fusion | flops 2717908992 | bytes 4718592 | tf_op jit(solution)/shard_map/dot_general | solution.py:58
  181.0 3.1 fusion.56
  184.1 2.1 copy.41
  186.2 2.1 fusion.6.a_ref
  188.3 61.6 %shard_map.209 = f32[384,384]{1,0:T(8,128)} custom-call(f32[384,384]{1,0:T(8,128)} %fusion.6.a_ref), custom_call_target="tpu_custom_call" | custom-call | tf_op jit(solution)/shard_map/pallas_call | solution.py:143
  250.0 3.5 fusion.57
  253.5 3.9 %fusion.58 = f32[768,384]{1,0:T(8,128)S(1)} fusion(f32[768,768]{1,0:T(8,128)S(1)} %bitcast.129, f32[768,384]{1,0:T(8,128)S(1)} %fusion.57), kind=kOutput, calls=%fused_computation.87 | convolution fusion | flops 2717908992 | bytes 4718592 | tf_op jit(solution)/shard_map/dot_general | solution.py:62
  257.3 3.8 %fusion.59 = f32[768,384]{1,0:T(8,128)S(1)} fusion(f32[768,768]{1,0:T(8,128)S(1)} %bitcast.130, f32[768,384]{1,0:T(8,128)S(1)} %fusion.58), kind=kOutput, calls=%fused_computation.88 | convolution fusion | flops 2717908992 | bytes 4718592 | tf_op jit(solution)/shard_map/dot_general | solution.py:58
  261.2 3.1 fusion.60
  264.3 2.1 copy.42
  266.4 2.1 fusion.5.a_ref
  268.5 61.6 %shard_map.210 = f32[384,384]{1,0:T(8,128)} custom-call(f32[384,384]{1,0:T(8,128)} %fusion.5.a_ref), custom_call_target="tpu_custom_call" | custom-call | tf_op jit(solution)/shard_map/pallas_call | solution.py:143
  330.2 3.1 fusion.61
  333.3 1.2 fusion.11
  334.5 0.0 copy-done
  334.5 2.4 collective-permute-start.5
  336.9 1.6 copy.43
  338.6 0.3 reshape.1091
  338.9 0.0 collective-permute-done.5
  338.9 1.5 convolution_bitcast_fusion.1
  (21 shorter events, 0.3 us)
Async XLA Ops:
  6.5 71.4 %all-gather.2.cloned.1.call-start = ((), (), s32[]{:S(2)}) async-start(), calls=%async_computation | async-start | bytes 2506752 | tf_op jit(solution)/shard_map/all_gather | solution.py:188
  8.2 26.0 %collective-permute-start = (f32[1,24,384]{2,1,0:T(8,128)}, f32[1,24,384]{2,1,0:T(8,128)S(1)}, u32[]{:S(2)}, u32[]{:S(2)}) collective-permute-start(f32[1,24,384]{2,1,0:T(8,128)} %bitcast.143), channel_id=1, source_target_pairs={{0,256},{16,272},{32,288},{48,304},{64,320},{80,336},{96,352},{112... | collective-permute-start | bytes 110600 | tf_op jit(solution)/shard_map/ppermute | solution.py:171
  35.1 14.3 %collective-permute-start.1 = (f32[2,1,24,384]{3,2,0,1:T(8,128)S(1)}, f32[2,1,24,384]{3,2,0,1:T(8,128)S(1)}, u32[]{:S(2)}, u32[]{:S(2)}) collective-permute-start(f32[2,1,24,384]{3,2,0,1:T(8,128)S(1)} %maximum_select_fusion.5), channel_id=1, source_target_pairs={{0,128},{16,144},{32,160},{48,176},{64,192},{80,208},{96,224},{112... | collective-permute-start | bytes 221192 | tf_op jit(solution)/shard_map/ppermute | solution.py:171
  49.3 10.6 %collective-permute-start.2 = (f32[2,2,1,24,384]{4,3,0,1,2:T(8,128)S(1)}, f32[2,2,1,24,384]{4,3,0,1,2:T(8,128)S(1)}, u32[]{:S(2)}, u32[]{:S(2)}) collective-permute-start(f32[2,2,1,24,384]{4,3,0,1,2:T(8,128)S(1)} %maximum_select_fusion.4), channel_id=1, source_target_pairs={{0,64},{16,80},{32,96},{48,112},{64,0},{80,16},{96,32},{112,48},{1... | collective-permute-start | bytes 442376 | tf_op jit(solution)/shard_map/ppermute | solution.py:171
  60.0 10.1 %collective-permute-start.3 = (f32[2,2,2,1,24,384]{5,4,0,1,2,3:T(8,128)S(1)}, f32[2,2,2,1,24,384]{5,4,0,1,2,3:T(8,128)S(1)}, u32[]{:S(2)}, u32[]{:S(2)}) collective-permute-start(f32[2,2,2,1,24,384]{5,4,0,1,2,3:T(8,128)S(1)} %maximum_select_fusion.3), channel_id=1, source_target_pairs={{0,32},{16,48},{32,0},{48,16},{64,96},{80,112},{96,64},{112,80},{1... | collective-permute-start | bytes 884744 | tf_op jit(solution)/shard_map/ppermute | solution.py:171
  62.0 11.3 %copy-start.4 = (f32[4,4]{1,0:T(4,128)S(1)}, f32[4,4]{1,0:T(4,128)}, u32[]{:S(2)}) copy-start(f32[4,4]{1,0:T(4,128)} %constant.56.clone) | copy-start | bytes 196
  62.0 11.3 %copy-start.5 = (f32[4,4]{1,0:T(4,128)S(1)}, f32[4,4]{1,0:T(4,128)}, u32[]{:S(2)}) copy-start(f32[4,4]{1,0:T(4,128)} %constant.55.clone) | copy-start | bytes 196
  62.0 11.3 %copy-start.8 = (f32[4,4]{1,0:T(4,128)S(1)}, f32[4,4]{1,0:T(4,128)}, u32[]{:S(2)}) copy-start(f32[4,4]{1,0:T(4,128)} %constant.58.clone) | copy-start | bytes 196
  62.0 14.3 %copy-start.2 = (f32[4,4]{1,0:T(4,128)S(1)}, f32[4,4]{1,0:T(4,128)}, u32[]{:S(2)}) copy-start(f32[4,4]{1,0:T(4,128)} %constant.60.clone) | copy-start | bytes 196
  62.0 14.3 %copy-start.3 = (f32[4,4]{1,0:T(4,128)S(1)}, f32[4,4]{1,0:T(4,128)}, u32[]{:S(2)}) copy-start(f32[4,4]{1,0:T(4,128)} %constant.59.clone) | copy-start | bytes 196
  62.0 14.3 %copy-start.7 = (f32[4,4]{1,0:T(4,128)S(1)}, f32[4,4]{1,0:T(4,128)}, u32[]{:S(2)}) copy-start(f32[4,4]{1,0:T(4,128)} %constant.61.clone) | copy-start | bytes 196
  62.1 14.4 %copy-start.6 = (f32[4,4]{1,0:T(4,128)S(1)}, f32[4,4]{1,0:T(4,128)}, u32[]{:S(2)}) copy-start(f32[4,4]{1,0:T(4,128)} %constant.62.clone) | copy-start | bytes 196
  70.1 6.6 %collective-permute-start.4 = (f32[2,2,2,2,1,24,384]{6,5,1,2,3,4,0:T(8,128)S(1)}, f32[2,2,2,2,1,24,384]{6,5,1,2,3,4,0:T(8,128)S(1)}, u32[]{:S(2)}, u32[]{:S(2)}) collective-permute-start(f32[2,2,2,2,1,24,384]{6,5,1,2,3,4,0:T(8,128)S(1)} %maximum_select_fusion.1), channel_id=1, source_target_pairs={{0,16},{16,0},{32,48},{48,32},{64,80},{80,64},{96,112},{112,96},{1... | collective-permute-start | bytes 1769480 | tf_op jit(solution)/shard_map/ppermute | solution.py:171
  95.5 1.3 copy-start.1
  333.3 1.2 copy-start
  334.5 4.4 %collective-permute-start.5 = (f32[24,768]{1,0:T(8,128)S(1)}, f32[24,768]{1,0:T(8,128)S(1)}, u32[]{:S(2)}, u32[]{:S(2)}) collective-permute-start(f32[24,768]{1,0:T(8,128)S(1)} %fusion.11), channel_id=1, source_target_pairs={{0,16},{16,32},{32,48},{48,64},{64,80},{80,96},{96,112},{112,128},... | collective-permute-start | bytes 221192 | tf_op jit(solution)/shard_map/ppermute | solution.py:19
Sparse Core Ops, SparseCore 0:
  10.3 64.6 all-gather.1
